TPU v7x, 32 devices: a whole 2x2x4 slice. The times are simulated.
32 devices in a mesh: section: 4 (over y, x), expert: 8 (over z, core).
Axes of the slice: x: 2, y: 2, z: 4, core: 2. Of those that a mesh axis runs over, the one named last changes fastest.
Arguments:
- layer_inputs: bfloat16 [4, 16, 64, 4096], P('section', None, 'expert'), may hold values from -6 to 6
- expert_ids: int32 [4, 16, 64, 2], P('section', None, 'expert'), may hold values from 0 to 7, all different within a row; in each aligned block of 8 rows (0 to 7, 8 to 15, ..., all dimensions but the last counted through in order) at most 3 rows name the same one
- gates: bfloat16 [4, 16, 64, 2], P('section', None, 'expert'), may hold values from 0.099609375 to 0.59765625
- w_gate: bfloat16 [4, 4096, 4096], P('section', None, 'expert'), may hold values from -0.09375 to 0.09375
- w_up: bfloat16 [4, 4096, 4096], P('section', None, 'expert'), may hold values from -0.09375 to 0.09375
- w_down: bfloat16 [4, 4096, 4096], P('section', 'expert'), may hold values from -0.25 to 0.25
- out_grad: bfloat16 [16, 64, 4096], P(None, 'expert'), may hold values from -6 to 6
Outputs:
- section_grads: bfloat16 [4, 16, 64, 4096], P('section', None, 'expert')
Inputs may be any that keep to these rules, and one draw needn't show every extreme that they name: `expert_ids`: within one micro-batch of one section, the 8 tokens of one expert index name each expert at most 3 times, and in some such groups one expert exactly 3 times; a token's 2 experts differ.
All inputs are finite; a program needn't handle non-finite values.
Results may differ from a plain program's by a relative error of at most 0.035.
Values may be sent and summed in bfloat16 or wider, within the bound.
No kernel may reach another device: no remote copies, remote signals or barrier semaphores. Data moves between devices by JAX's collectives and lax.ppermute only.
A program may use at most 64 MiB of HBM per device.

v0:
```python
import jax
import jax.numpy as jnp
from jax import lax
from jax.sharding import PartitionSpec as P

EXPERTS = 8
CAP = 3


def passed_along(x, axis, by):
    length = lax.axis_size(axis)
    pairs = [(i, i + by) for i in range(length) if 0 <= i + by < length]
    return lax.ppermute(x, axis, pairs)


def selection(choices, capacity):
    token_count, top_count = (choices.shape[-2], choices.shape[-1])
    experts = jnp.arange(EXPERTS, dtype=jnp.int32)
    onehot = (choices[..., None] == experts).astype(jnp.int32)
    leading = onehot.shape[:-3]
    flattened = onehot.reshape(leading + (token_count * top_count, EXPERTS))
    before = jnp.cumsum(flattened, axis=-2) - flattened
    slot_index = jnp.sum((before * flattened).reshape(onehot.shape), axis=-1)
    places = jnp.arange(capacity, dtype=jnp.int32)
    in_slot = (slot_index[..., None] == places).astype(jnp.int32)
    return onehot[..., None] * in_slot[..., None, :]


def on_device(layer_inputs, expert_ids, gates, w_gate, w_up, w_down, out_grad):
    expert_count = lax.axis_size("expert")
    section_count = lax.axis_size("section")
    section_index = lax.axis_index("section")
    inputs = layer_inputs[0]
    gate_slice = w_gate[0]
    up_slice = w_up[0]
    down_slice = w_down[0]
    micro_count, token_count, model_width = inputs.shape
    hidden = gate_slice.shape[1]
    shards = expert_count // EXPERTS
    capacity = CAP
    slot_rows = expert_count * capacity
    contract = (((1,), (1,)), ((), ()))
    selected = selection(expert_ids[0], capacity)
    dispatch = jnp.sum(selected, axis=2).astype(jnp.bfloat16)
    gate_values = gates[0].astype(jnp.float32)
    combine = jnp.sum(selected.astype(jnp.float32) * gate_values[..., None, None], axis=2).astype(
        jnp.bfloat16
    )

    def spread(rows):
        leading = rows.shape[:-3]
        rows = rows.astype(jnp.bfloat16)
        rows = jnp.broadcast_to(
            jnp.expand_dims(rows, -3), leading + (EXPERTS, shards, capacity, model_width)
        )
        return rows.reshape(leading + (expert_count, capacity, model_width))

    def backward_rows(grad_block, act, coef):
        down_grad = lax.dot_general(
            grad_block, down_slice, contract, preferred_element_type=jnp.float32
        )
        dgate = (down_grad * coef).astype(jnp.bfloat16)
        dup = (down_grad * act).astype(jnp.bfloat16)
        total = lax.dot_general(dgate, gate_slice, contract, preferred_element_type=jnp.float32)
        total = total + lax.dot_general(dup, up_slice, contract, preferred_element_type=jnp.float32)
        return total.astype(jnp.bfloat16)

    zeros_back = jnp.zeros((slot_rows, model_width), jnp.bfloat16)
    outgoing = spread(
        jnp.einsum("mtec,mtd->mecd", dispatch, inputs, preferred_element_type=jnp.float32)
    )
    received = lax.all_to_all(outgoing, "expert", split_axis=1, concat_axis=1, tiled=True)
    item_count = received.shape[0]
    row_block = received.reshape(-1, model_width)
    pre_gate = jnp.dot(row_block, gate_slice, preferred_element_type=jnp.float32)
    pre_up = jnp.dot(row_block, up_slice, preferred_element_type=jnp.float32)
    sigmoid_gate = jax.nn.sigmoid(pre_gate)
    act = pre_gate * sigmoid_gate
    coef = pre_up * (sigmoid_gate * (1.0 + pre_gate * (1.0 - sigmoid_gate)))
    act, coef = (act, coef)
    saved = jnp.stack([act, coef]).reshape(2, item_count, slot_rows, hidden)
    act_all = saved[0]
    coef_all = saved[1]

    def tick(tick_index, state_pair):
        incoming, results = state_pair
        micro_index = tick_index - (section_count - 1 - section_index)
        active = (micro_index >= 0) & (micro_index < micro_count)
        micro_slot = jnp.clip(micro_index, 0, micro_count - 1)
        top_grad = lax.dynamic_index_in_dim(out_grad, micro_slot, 0, keepdims=False)
        grad_out = jnp.where(section_index == section_count - 1, top_grad, incoming)
        dispatch_micro = lax.dynamic_index_in_dim(dispatch, micro_slot, 0, keepdims=False)
        combine_micro = lax.dynamic_index_in_dim(combine, micro_slot, 0, keepdims=False)
        grad_rows = spread(
            jnp.einsum("tec,td->ecd", dispatch_micro, grad_out, preferred_element_type=jnp.float32)
        )
        arrived = lax.all_to_all(
            grad_rows, "expert", split_axis=0, concat_axis=0, tiled=True
        ).reshape(slot_rows, model_width)

        def local_saved(row_block):
            act = lax.dynamic_index_in_dim(act_all, micro_slot, 0, keepdims=False)
            coef = lax.dynamic_index_in_dim(coef_all, micro_slot, 0, keepdims=False)
            return backward_rows(row_block, act, coef)

        def skip_saved(row_block):
            return zeros_back

        back = lax.cond(active, local_saved, skip_saved, arrived)
        returned = lax.all_to_all(
            back.reshape(expert_count, capacity, model_width),
            "expert",
            split_axis=0,
            concat_axis=0,
            tiled=True,
        )
        returned = returned.reshape(EXPERTS, shards, capacity, model_width)
        mixed = jnp.einsum(
            "tec,ekcd->td", combine_micro, returned, preferred_element_type=jnp.float32
        )
        grad_in = (grad_out.astype(jnp.float32) + mixed).astype(jnp.bfloat16)
        updated = lax.dynamic_update_index_in_dim(results, grad_in, micro_slot, 0)
        results = jnp.where(active, updated, results)
        passed = passed_along(grad_in, "section", -1)
        return (passed, results)

    initial = (
        jnp.zeros((token_count, model_width), jnp.bfloat16),
        jnp.zeros((micro_count, token_count, model_width), jnp.bfloat16),
    )
    final_state = lax.fori_loop(0, micro_count + section_count - 1, tick, initial)
    return final_state[1][None]


def solution(mesh):
    placed = (
        P("section", None, "expert", None),
        P("section", None, "expert", None),
        P("section", None, "expert", None),
        P("section", None, "expert"),
        P("section", None, "expert"),
        P("section", "expert", None),
        P(None, "expert", None),
    )
    return jax.shard_map(
        on_device,
        mesh=mesh,
        in_specs=placed,
        out_specs=P("section", None, "expert", None),
        check_vma=False,
    )
```

profile of v0, /device:TPU:0, one launch (start us, length us, event | category | flops | bytes accessed | tf_op | source)
XLA Modules:
  0.0 926.5 jit_solution(10920918957178895097)
XLA Ops:
  13.3 71.5 %all-to-all-done.2 = bf16[16,8,3,4096]{3,0,2,1:T(8,128)(2,1)} async-done(((bf16[16,8,3,4096]{3,0,2,1:T(8,128)(2,1)}), bf16[16,8,3,4096]{3,0,2,1:T(8,128)(2,1)}, u32[]{:S(2)}, u32[]{:S(2)}) %all-to-all-start.2) | async-done | bytes 3145760 | tf_op jit(solution)/shard_map/all_to_all | solution.py:72
  107.7 817.8 %while.17 = (s32[]{:T(128)}, bf16[8,4096]{1,0:T(8,128)(2,1)S(1)}, bf16[16,8,4096]{2,1,0:T(8,128)(2,1)S(1)}, pred[]{:T(512)}, s32[]{:T(128)}, /*index=5*/bf16[16,...) while((s32[]{:T(128)}, bf16[8,4096]{1,0:T(8,128)(2,1)S(1)}, ...), condition=%wide.region_7.8_spmd, body=%wide.region_4.7_spmd.sunk | while | flops 305676288 | bytes 51051968 | solution.py:131
  113.0 9.7 %all-to-all-done = bf16[8,3,4096]{2,1,0:T(4,128)(2,1)S(1)} async-done(((bf16[8,3,4096]{2,1,0:T(4,128)(2,1)}), bf16[8,3,4096]{2,1,0:T(4,128)(2,1)S(1)}, u32[]{:S(2)}, u32[]{:S(2)}) %all-to-all-start) | async-done | bytes 196640 | tf_op jit(solution)/shard_map/while/body/eval_jaxpr/all_to_all | solution.py:97
  122.9 12.1 %all_to_all.29 = bf16[8,3,4096]{2,1,0:T(4,128)(2,1)S(1)} all-to-all(bf16[8,3,4096]{2,1,0:T(4,128)(2,1)S(1)} %reshape.67), channel_id=1, replica_groups=mesh['section'=4,'expert'=8] {'expert'}, dimensions={0} | all-to-all | bytes 393216 | tf_op jit(solution)/shard_map/while/body/eval_jaxpr/all_to_all | solution.py:110
  147.6 9.7 %all-to-all-done = bf16[8,3,4096]{2,1,0:T(4,128)(2,1)S(1)} async-done(((bf16[8,3,4096]{2,1,0:T(4,128)(2,1)}), bf16[8,3,4096]{2,1,0:T(4,128)(2,1)S(1)}, u32[]{:S(2)}, u32[]{:S(2)}) %all-to-all-start) | async-done | bytes 196640 | tf_op jit(solution)/shard_map/while/body/eval_jaxpr/all_to_all | solution.py:97
  157.4 12.1 %all_to_all.29 = bf16[8,3,4096]{2,1,0:T(4,128)(2,1)S(1)} all-to-all(bf16[8,3,4096]{2,1,0:T(4,128)(2,1)S(1)} %reshape.67), channel_id=1, replica_groups=mesh['section'=4,'expert'=8] {'expert'}, dimensions={0} | all-to-all | bytes 393216 | tf_op jit(solution)/shard_map/while/body/eval_jaxpr/all_to_all | solution.py:110
  182.5 9.7 %all-to-all-done = bf16[8,3,4096]{2,1,0:T(4,128)(2,1)S(1)} async-done(((bf16[8,3,4096]{2,1,0:T(4,128)(2,1)}), bf16[8,3,4096]{2,1,0:T(4,128)(2,1)S(1)}, u32[]{:S(2)}, u32[]{:S(2)}) %all-to-all-start) | async-done | bytes 196640 | tf_op jit(solution)/shard_map/while/body/eval_jaxpr/all_to_all | solution.py:97
  192.3 12.1 %all_to_all.29 = bf16[8,3,4096]{2,1,0:T(4,128)(2,1)S(1)} all-to-all(bf16[8,3,4096]{2,1,0:T(4,128)(2,1)S(1)} %reshape.67), channel_id=1, replica_groups=mesh['section'=4,'expert'=8] {'expert'}, dimensions={0} | all-to-all | bytes 393216 | tf_op jit(solution)/shard_map/while/body/eval_jaxpr/all_to_all | solution.py:110
  206.9 26.0 %collective-permute-done = bf16[8,4096]{1,0:T(8,128)(2,1)S(1)} collective-permute-done((bf16[8,4096]{1,0:T(8,128)(2,1)S(1)}, bf16[8,4096]{1,0:T(8,128)(2,1)S(1)}, u32[]{:S(2)}, u32[]{:S(2)}) %collective-permute-start) | collective-permute-done | bytes 65568 | tf_op jit(solution)/shard_map/while/body/eval_jaxpr/ppermute | solution.py:13
  238.2 9.7 %all-to-all-done = bf16[8,3,4096]{2,1,0:T(4,128)(2,1)S(1)} async-done(((bf16[8,3,4096]{2,1,0:T(4,128)(2,1)}), bf16[8,3,4096]{2,1,0:T(4,128)(2,1)S(1)}, u32[]{:S(2)}, u32[]{:S(2)}) %all-to-all-start) | async-done | bytes 196640 | tf_op jit(solution)/shard_map/while/body/eval_jaxpr/all_to_all | solution.py:97
  247.8 7.9 conditional.2
  255.9 12.1 %all_to_all.29 = bf16[8,3,4096]{2,1,0:T(4,128)(2,1)S(1)} all-to-all(bf16[8,3,4096]{2,1,0:T(4,128)(2,1)S(1)} %reshape.67), channel_id=1, replica_groups=mesh['section'=4,'expert'=8] {'expert'}, dimensions={0} | all-to-all | bytes 393216 | tf_op jit(solution)/shard_map/while/body/eval_jaxpr/all_to_all | solution.py:110
  281.5 9.7 %all-to-all-done = bf16[8,3,4096]{2,1,0:T(4,128)(2,1)S(1)} async-done(((bf16[8,3,4096]{2,1,0:T(4,128)(2,1)}), bf16[8,3,4096]{2,1,0:T(4,128)(2,1)S(1)}, u32[]{:S(2)}, u32[]{:S(2)}) %all-to-all-start) | async-done | bytes 196640 | tf_op jit(solution)/shard_map/while/body/eval_jaxpr/all_to_all | solution.py:97
  291.2 7.9 conditional.2
  299.2 12.1 %all_to_all.29 = bf16[8,3,4096]{2,1,0:T(4,128)(2,1)S(1)} all-to-all(bf16[8,3,4096]{2,1,0:T(4,128)(2,1)S(1)} %reshape.67), channel_id=1, replica_groups=mesh['section'=4,'expert'=8] {'expert'}, dimensions={0} | all-to-all | bytes 393216 | tf_op jit(solution)/shard_map/while/body/eval_jaxpr/all_to_all | solution.py:110
  324.9 9.7 %all-to-all-done = bf16[8,3,4096]{2,1,0:T(4,128)(2,1)S(1)} async-done(((bf16[8,3,4096]{2,1,0:T(4,128)(2,1)}), bf16[8,3,4096]{2,1,0:T(4,128)(2,1)S(1)}, u32[]{:S(2)}, u32[]{:S(2)}) %all-to-all-start) | async-done | bytes 196640 | tf_op jit(solution)/shard_map/while/body/eval_jaxpr/all_to_all | solution.py:97
  342.6 12.1 %all_to_all.29 = bf16[8,3,4096]{2,1,0:T(4,128)(2,1)S(1)} all-to-all(bf16[8,3,4096]{2,1,0:T(4,128)(2,1)S(1)} %reshape.67), channel_id=1, replica_groups=mesh['section'=4,'expert'=8] {'expert'}, dimensions={0} | all-to-all | bytes 393216 | tf_op jit(solution)/shard_map/while/body/eval_jaxpr/all_to_all | solution.py:110
  368.2 9.7 %all-to-all-done = bf16[8,3,4096]{2,1,0:T(4,128)(2,1)S(1)} async-done(((bf16[8,3,4096]{2,1,0:T(4,128)(2,1)}), bf16[8,3,4096]{2,1,0:T(4,128)(2,1)S(1)}, u32[]{:S(2)}, u32[]{:S(2)}) %all-to-all-start) | async-done | bytes 196640 | tf_op jit(solution)/shard_map/while/body/eval_jaxpr/all_to_all | solution.py:97
  385.9 12.1 %all_to_all.29 = bf16[8,3,4096]{2,1,0:T(4,128)(2,1)S(1)} all-to-all(bf16[8,3,4096]{2,1,0:T(4,128)(2,1)S(1)} %reshape.67), channel_id=1, replica_groups=mesh['section'=4,'expert'=8] {'expert'}, dimensions={0} | all-to-all | bytes 393216 | tf_op jit(solution)/shard_map/while/body/eval_jaxpr/all_to_all | solution.py:110
  411.6 9.7 %all-to-all-done = bf16[8,3,4096]{2,1,0:T(4,128)(2,1)S(1)} async-done(((bf16[8,3,4096]{2,1,0:T(4,128)(2,1)}), bf16[8,3,4096]{2,1,0:T(4,128)(2,1)S(1)}, u32[]{:S(2)}, u32[]{:S(2)}) %all-to-all-start) | async-done | bytes 196640 | tf_op jit(solution)/shard_map/while/body/eval_jaxpr/all_to_all | solution.py:97
  429.3 12.1 %all_to_all.29 = bf16[8,3,4096]{2,1,0:T(4,128)(2,1)S(1)} all-to-all(bf16[8,3,4096]{2,1,0:T(4,128)(2,1)S(1)} %reshape.67), channel_id=1, replica_groups=mesh['section'=4,'expert'=8] {'expert'}, dimensions={0} | all-to-all | bytes 393216 | tf_op jit(solution)/shard_map/while/body/eval_jaxpr/all_to_all | solution.py:110
  454.9 9.7 %all-to-all-done = bf16[8,3,4096]{2,1,0:T(4,128)(2,1)S(1)} async-done(((bf16[8,3,4096]{2,1,0:T(4,128)(2,1)}), bf16[8,3,4096]{2,1,0:T(4,128)(2,1)S(1)}, u32[]{:S(2)}, u32[]{:S(2)}) %all-to-all-start) | async-done | bytes 196640 | tf_op jit(solution)/shard_map/while/body/eval_jaxpr/all_to_all | solution.py:97
  464.6 7.9 conditional.2
  472.6 12.1 %all_to_all.29 = bf16[8,3,4096]{2,1,0:T(4,128)(2,1)S(1)} all-to-all(bf16[8,3,4096]{2,1,0:T(4,128)(2,1)S(1)} %reshape.67), channel_id=1, replica_groups=mesh['section'=4,'expert'=8] {'expert'}, dimensions={0} | all-to-all | bytes 393216 | tf_op jit(solution)/shard_map/while/body/eval_jaxpr/all_to_all | solution.py:110
  498.3 9.7 %all-to-all-done = bf16[8,3,4096]{2,1,0:T(4,128)(2,1)S(1)} async-done(((bf16[8,3,4096]{2,1,0:T(4,128)(2,1)}), bf16[8,3,4096]{2,1,0:T(4,128)(2,1)S(1)}, u32[]{:S(2)}, u32[]{:S(2)}) %all-to-all-start) | async-done | bytes 196640 | tf_op jit(solution)/shard_map/while/body/eval_jaxpr/all_to_all | solution.py:97
  507.9 7.9 conditional.2
  516.0 12.1 %all_to_all.29 = bf16[8,3,4096]{2,1,0:T(4,128)(2,1)S(1)} all-to-all(bf16[8,3,4096]{2,1,0:T(4,128)(2,1)S(1)} %reshape.67), channel_id=1, replica_groups=mesh['section'=4,'expert'=8] {'expert'}, dimensions={0} | all-to-all | bytes 393216 | tf_op jit(solution)/shard_map/while/body/eval_jaxpr/all_to_all | solution.py:110
  541.6 9.7 %all-to-all-done = bf16[8,3,4096]{2,1,0:T(4,128)(2,1)S(1)} async-done(((bf16[8,3,4096]{2,1,0:T(4,128)(2,1)}), bf16[8,3,4096]{2,1,0:T(4,128)(2,1)S(1)}, u32[]{:S(2)}, u32[]{:S(2)}) %all-to-all-start) | async-done | bytes 196640 | tf_op jit(solution)/shard_map/while/body/eval_jaxpr/all_to_all | solution.py:97
  559.3 12.1 %all_to_all.29 = bf16[8,3,4096]{2,1,0:T(4,128)(2,1)S(1)} all-to-all(bf16[8,3,4096]{2,1,0:T(4,128)(2,1)S(1)} %reshape.67), channel_id=1, replica_groups=mesh['section'=4,'expert'=8] {'expert'}, dimensions={0} | all-to-all | bytes 393216 | tf_op jit(solution)/shard_map/while/body/eval_jaxpr/all_to_all | solution.py:110
  585.0 9.7 %all-to-all-done = bf16[8,3,4096]{2,1,0:T(4,128)(2,1)S(1)} async-done(((bf16[8,3,4096]{2,1,0:T(4,128)(2,1)}), bf16[8,3,4096]{2,1,0:T(4,128)(2,1)S(1)}, u32[]{:S(2)}, u32[]{:S(2)}) %all-to-all-start) | async-done | bytes 196640 | tf_op jit(solution)/shard_map/while/body/eval_jaxpr/all_to_all | solution.py:97
  602.7 12.1 %all_to_all.29 = bf16[8,3,4096]{2,1,0:T(4,128)(2,1)S(1)} all-to-all(bf16[8,3,4096]{2,1,0:T(4,128)(2,1)S(1)} %reshape.67), channel_id=1, replica_groups=mesh['section'=4,'expert'=8] {'expert'}, dimensions={0} | all-to-all | bytes 393216 | tf_op jit(solution)/shard_map/while/body/eval_jaxpr/all_to_all | solution.py:110
  628.3 9.7 %all-to-all-done = bf16[8,3,4096]{2,1,0:T(4,128)(2,1)S(1)} async-done(((bf16[8,3,4096]{2,1,0:T(4,128)(2,1)}), bf16[8,3,4096]{2,1,0:T(4,128)(2,1)S(1)}, u32[]{:S(2)}, u32[]{:S(2)}) %all-to-all-start) | async-done | bytes 196640 | tf_op jit(solution)/shard_map/while/body/eval_jaxpr/all_to_all | solution.py:97
  638.0 7.9 conditional.2
  646.0 12.1 %all_to_all.29 = bf16[8,3,4096]{2,1,0:T(4,128)(2,1)S(1)} all-to-all(bf16[8,3,4096]{2,1,0:T(4,128)(2,1)S(1)} %reshape.67), channel_id=1, replica_groups=mesh['section'=4,'expert'=8] {'expert'}, dimensions={0} | all-to-all | bytes 393216 | tf_op jit(solution)/shard_map/while/body/eval_jaxpr/all_to_all | solution.py:110
  671.7 9.7 %all-to-all-done = bf16[8,3,4096]{2,1,0:T(4,128)(2,1)S(1)} async-done(((bf16[8,3,4096]{2,1,0:T(4,128)(2,1)}), bf16[8,3,4096]{2,1,0:T(4,128)(2,1)S(1)}, u32[]{:S(2)}, u32[]{:S(2)}) %all-to-all-start) | async-done | bytes 196640 | tf_op jit(solution)/shard_map/while/body/eval_jaxpr/all_to_all | solution.py:97
  689.4 12.1 %all_to_all.29 = bf16[8,3,4096]{2,1,0:T(4,128)(2,1)S(1)} all-to-all(bf16[8,3,4096]{2,1,0:T(4,128)(2,1)S(1)} %reshape.67), channel_id=1, replica_groups=mesh['section'=4,'expert'=8] {'expert'}, dimensions={0} | all-to-all | bytes 393216 | tf_op jit(solution)/shard_map/while/body/eval_jaxpr/all_to_all | solution.py:110
  715.0 9.7 %all-to-all-done = bf16[8,3,4096]{2,1,0:T(4,128)(2,1)S(1)} async-done(((bf16[8,3,4096]{2,1,0:T(4,128)(2,1)}), bf16[8,3,4096]{2,1,0:T(4,128)(2,1)S(1)}, u32[]{:S(2)}, u32[]{:S(2)}) %all-to-all-start) | async-done | bytes 196640 | tf_op jit(solution)/shard_map/while/body/eval_jaxpr/all_to_all | solution.py:97
  724.7 7.9 conditional.2
  732.7 12.1 %all_to_all.29 = bf16[8,3,4096]{2,1,0:T(4,128)(2,1)S(1)} all-to-all(bf16[8,3,4096]{2,1,0:T(4,128)(2,1)S(1)} %reshape.67), channel_id=1, replica_groups=mesh['section'=4,'expert'=8] {'expert'}, dimensions={0} | all-to-all | bytes 393216 | tf_op jit(solution)/shard_map/while/body/eval_jaxpr/all_to_all | solution.py:110
  758.3 9.7 %all-to-all-done = bf16[8,3,4096]{2,1,0:T(4,128)(2,1)S(1)} async-done(((bf16[8,3,4096]{2,1,0:T(4,128)(2,1)}), bf16[8,3,4096]{2,1,0:T(4,128)(2,1)S(1)}, u32[]{:S(2)}, u32[]{:S(2)}) %all-to-all-start) | async-done | bytes 196640 | tf_op jit(solution)/shard_map/while/body/eval_jaxpr/all_to_all | solution.py:97
  776.1 12.1 %all_to_all.29 = bf16[8,3,4096]{2,1,0:T(4,128)(2,1)S(1)} all-to-all(bf16[8,3,4096]{2,1,0:T(4,128)(2,1)S(1)} %reshape.67), channel_id=1, replica_groups=mesh['section'=4,'expert'=8] {'expert'}, dimensions={0} | all-to-all | bytes 393216 | tf_op jit(solution)/shard_map/while/body/eval_jaxpr/all_to_all | solution.py:110
  801.7 9.7 %all-to-all-done = bf16[8,3,4096]{2,1,0:T(4,128)(2,1)S(1)} async-done(((bf16[8,3,4096]{2,1,0:T(4,128)(2,1)}), bf16[8,3,4096]{2,1,0:T(4,128)(2,1)S(1)}, u32[]{:S(2)}, u32[]{:S(2)}) %all-to-all-start) | async-done | bytes 196640 | tf_op jit(solution)/shard_map/while/body/eval_jaxpr/all_to_all | solution.py:97
  811.3 7.9 conditional.2
  819.4 12.1 %all_to_all.29 = bf16[8,3,4096]{2,1,0:T(4,128)(2,1)S(1)} all-to-all(bf16[8,3,4096]{2,1,0:T(4,128)(2,1)S(1)} %reshape.67), channel_id=1, replica_groups=mesh['section'=4,'expert'=8] {'expert'}, dimensions={0} | all-to-all | bytes 393216 | tf_op jit(solution)/shard_map/while/body/eval_jaxpr/all_to_all | solution.py:110
  845.0 9.7 %all-to-all-done = bf16[8,3,4096]{2,1,0:T(4,128)(2,1)S(1)} async-done(((bf16[8,3,4096]{2,1,0:T(4,128)(2,1)}), bf16[8,3,4096]{2,1,0:T(4,128)(2,1)S(1)}, u32[]{:S(2)}, u32[]{:S(2)}) %all-to-all-start) | async-done | bytes 196640 | tf_op jit(solution)/shard_map/while/body/eval_jaxpr/all_to_all | solution.py:97
  862.7 12.1 %all_to_all.29 = bf16[8,3,4096]{2,1,0:T(4,128)(2,1)S(1)} all-to-all(bf16[8,3,4096]{2,1,0:T(4,128)(2,1)S(1)} %reshape.67), channel_id=1, replica_groups=mesh['section'=4,'expert'=8] {'expert'}, dimensions={0} | all-to-all | bytes 393216 | tf_op jit(solution)/shard_map/while/body/eval_jaxpr/all_to_all | solution.py:110
  888.4 9.7 %all-to-all-done = bf16[8,3,4096]{2,1,0:T(4,128)(2,1)S(1)} async-done(((bf16[8,3,4096]{2,1,0:T(4,128)(2,1)}), bf16[8,3,4096]{2,1,0:T(4,128)(2,1)S(1)}, u32[]{:S(2)}, u32[]{:S(2)}) %all-to-all-start) | async-done | bytes 196640 | tf_op jit(solution)/shard_map/while/body/eval_jaxpr/all_to_all | solution.py:97
  906.1 12.1 %all_to_all.29 = bf16[8,3,4096]{2,1,0:T(4,128)(2,1)S(1)} all-to-all(bf16[8,3,4096]{2,1,0:T(4,128)(2,1)S(1)} %reshape.67), channel_id=1, replica_groups=mesh['section'=4,'expert'=8] {'expert'}, dimensions={0} | all-to-all | bytes 393216 | tf_op jit(solution)/shard_map/while/body/eval_jaxpr/all_to_all | solution.py:110
  (303 shorter events, 484.3 us)
Async XLA Ops:
  6.7 6.5 copy-start.6
  6.7 78.1 %all-to-all-start.2 = ((bf16[16,8,3,4096]{3,0,2,1:T(8,128)(2,1)}), bf16[16,8,3,4096]{3,0,2,1:T(8,128)(2,1)}, u32[]{:S(2)}, u32[]{:S(2)}) async-start(bf16[16,8,3,4096]{3,0,2,1:T(8,128)(2,1)} %copy.34), calls=%async_computation.2 | async-start | bytes 6291456 | tf_op jit(solution)/shard_map/all_to_all | solution.py:72
  98.7 6.1 copy-start.2
  98.7 6.1 copy-start.4
  109.6 13.1 %all-to-all-start = ((bf16[8,3,4096]{2,1,0:T(4,128)(2,1)}), bf16[8,3,4096]{2,1,0:T(4,128)(2,1)S(1)}, u32[]{:S(2)}, u32[]{:S(2)}) async-start(bf16[8,3,4096]{2,1,0:T(4,128)(2,1)} %copy.46), calls=%async_computation | async-start | bytes 524288 | tf_op jit(solution)/shard_map/while/body/eval_jaxpr/all_to_all | solution.py:97
  136.1 6.2 collective-permute-start
  144.2 13.1 %all-to-all-start = ((bf16[8,3,4096]{2,1,0:T(4,128)(2,1)}), bf16[8,3,4096]{2,1,0:T(4,128)(2,1)S(1)}, u32[]{:S(2)}, u32[]{:S(2)}) async-start(bf16[8,3,4096]{2,1,0:T(4,128)(2,1)} %copy.46), calls=%async_computation | async-start | bytes 524288 | tf_op jit(solution)/shard_map/while/body/eval_jaxpr/all_to_all | solution.py:97
  170.7 6.5 collective-permute-start
  179.1 13.1 %all-to-all-start = ((bf16[8,3,4096]{2,1,0:T(4,128)(2,1)}), bf16[8,3,4096]{2,1,0:T(4,128)(2,1)S(1)}, u32[]{:S(2)}, u32[]{:S(2)}) async-start(bf16[8,3,4096]{2,1,0:T(4,128)(2,1)} %copy.46), calls=%async_computation | async-start | bytes 524288 | tf_op jit(solution)/shard_map/while/body/eval_jaxpr/all_to_all | solution.py:97
  205.6 27.3 %collective-permute-start = (bf16[8,4096]{1,0:T(8,128)(2,1)S(1)}, bf16[8,4096]{1,0:T(8,128)(2,1)S(1)}, u32[]{:S(2)}, u32[]{:S(2)}) collective-permute-start(bf16[8,4096]{1,0:T(8,128)(2,1)S(1)} %get-tuple-element.455), channel_id=1, source_target_pairs={{8,0},{16,8},{24,16},{9,1},{17,9},{25,17},{10,2},{18,10},{26,18},{... | collective-permute-start | bytes 196616 | tf_op jit(solution)/shard_map/while/body/eval_jaxpr/ppermute | solution.py:13
  234.8 13.1 %all-to-all-start = ((bf16[8,3,4096]{2,1,0:T(4,128)(2,1)}), bf16[8,3,4096]{2,1,0:T(4,128)(2,1)S(1)}, u32[]{:S(2)}, u32[]{:S(2)}) async-start(bf16[8,3,4096]{2,1,0:T(4,128)(2,1)} %copy.46), calls=%async_computation | async-start | bytes 524288 | tf_op jit(solution)/shard_map/while/body/eval_jaxpr/all_to_all | solution.py:97
  248.0 5.7 copy-start.3
  269.1 7.1 collective-permute-start
  278.1 13.1 %all-to-all-start = ((bf16[8,3,4096]{2,1,0:T(4,128)(2,1)}), bf16[8,3,4096]{2,1,0:T(4,128)(2,1)S(1)}, u32[]{:S(2)}, u32[]{:S(2)}) async-start(bf16[8,3,4096]{2,1,0:T(4,128)(2,1)} %copy.46), calls=%async_computation | async-start | bytes 524288 | tf_op jit(solution)/shard_map/while/body/eval_jaxpr/all_to_all | solution.py:97
  291.4 5.7 copy-start.3
  312.5 7.1 collective-permute-start
  321.5 13.1 %all-to-all-start = ((bf16[8,3,4096]{2,1,0:T(4,128)(2,1)}), bf16[8,3,4096]{2,1,0:T(4,128)(2,1)S(1)}, u32[]{:S(2)}, u32[]{:S(2)}) async-start(bf16[8,3,4096]{2,1,0:T(4,128)(2,1)} %copy.46), calls=%async_computation | async-start | bytes 524288 | tf_op jit(solution)/shard_map/while/body/eval_jaxpr/all_to_all | solution.py:97
  334.7 5.7 copy-start.3
  355.8 7.1 collective-permute-start
  364.8 13.1 %all-to-all-start = ((bf16[8,3,4096]{2,1,0:T(4,128)(2,1)}), bf16[8,3,4096]{2,1,0:T(4,128)(2,1)S(1)}, u32[]{:S(2)}, u32[]{:S(2)}) async-start(bf16[8,3,4096]{2,1,0:T(4,128)(2,1)} %copy.46), calls=%async_computation | async-start | bytes 524288 | tf_op jit(solution)/shard_map/while/body/eval_jaxpr/all_to_all | solution.py:97
  378.1 5.7 copy-start.3
  399.2 7.1 collective-permute-start
  408.1 13.1 %all-to-all-start = ((bf16[8,3,4096]{2,1,0:T(4,128)(2,1)}), bf16[8,3,4096]{2,1,0:T(4,128)(2,1)S(1)}, u32[]{:S(2)}, u32[]{:S(2)}) async-start(bf16[8,3,4096]{2,1,0:T(4,128)(2,1)} %copy.46), calls=%async_computation | async-start | bytes 524288 | tf_op jit(solution)/shard_map/while/body/eval_jaxpr/all_to_all | solution.py:97
  421.4 5.7 copy-start.3
  442.5 7.1 collective-permute-start
  451.5 13.1 %all-to-all-start = ((bf16[8,3,4096]{2,1,0:T(4,128)(2,1)}), bf16[8,3,4096]{2,1,0:T(4,128)(2,1)S(1)}, u32[]{:S(2)}, u32[]{:S(2)}) async-start(bf16[8,3,4096]{2,1,0:T(4,128)(2,1)} %copy.46), calls=%async_computation | async-start | bytes 524288 | tf_op jit(solution)/shard_map/while/body/eval_jaxpr/all_to_all | solution.py:97
  485.9 7.1 collective-permute-start
  494.8 13.1 %all-to-all-start = ((bf16[8,3,4096]{2,1,0:T(4,128)(2,1)}), bf16[8,3,4096]{2,1,0:T(4,128)(2,1)S(1)}, u32[]{:S(2)}, u32[]{:S(2)}) async-start(bf16[8,3,4096]{2,1,0:T(4,128)(2,1)} %copy.46), calls=%async_computation | async-start | bytes 524288 | tf_op jit(solution)/shard_map/while/body/eval_jaxpr/all_to_all | solution.py:97
  529.2 7.1 collective-permute-start
  538.2 13.1 %all-to-all-start = ((bf16[8,3,4096]{2,1,0:T(4,128)(2,1)}), bf16[8,3,4096]{2,1,0:T(4,128)(2,1)S(1)}, u32[]{:S(2)}, u32[]{:S(2)}) async-start(bf16[8,3,4096]{2,1,0:T(4,128)(2,1)} %copy.46), calls=%async_computation | async-start | bytes 524288 | tf_op jit(solution)/shard_map/while/body/eval_jaxpr/all_to_all | solution.py:97
  572.6 7.1 collective-permute-start
  581.5 13.1 %all-to-all-start = ((bf16[8,3,4096]{2,1,0:T(4,128)(2,1)}), bf16[8,3,4096]{2,1,0:T(4,128)(2,1)S(1)}, u32[]{:S(2)}, u32[]{:S(2)}) async-start(bf16[8,3,4096]{2,1,0:T(4,128)(2,1)} %copy.46), calls=%async_computation | async-start | bytes 524288 | tf_op jit(solution)/shard_map/while/body/eval_jaxpr/all_to_all | solution.py:97
  594.8 5.7 copy-start.3
  615.9 7.1 collective-permute-start
  624.9 13.1 %all-to-all-start = ((bf16[8,3,4096]{2,1,0:T(4,128)(2,1)}), bf16[8,3,4096]{2,1,0:T(4,128)(2,1)S(1)}, u32[]{:S(2)}, u32[]{:S(2)}) async-start(bf16[8,3,4096]{2,1,0:T(4,128)(2,1)} %copy.46), calls=%async_computation | async-start | bytes 524288 | tf_op jit(solution)/shard_map/while/body/eval_jaxpr/all_to_all | solution.py:97
  659.3 7.1 collective-permute-start
  668.2 13.1 %all-to-all-start = ((bf16[8,3,4096]{2,1,0:T(4,128)(2,1)}), bf16[8,3,4096]{2,1,0:T(4,128)(2,1)S(1)}, u32[]{:S(2)}, u32[]{:S(2)}) async-start(bf16[8,3,4096]{2,1,0:T(4,128)(2,1)} %copy.46), calls=%async_computation | async-start | bytes 524288 | tf_op jit(solution)/shard_map/while/body/eval_jaxpr/all_to_all | solution.py:97
  702.6 7.1 collective-permute-start
  711.6 13.1 %all-to-all-start = ((bf16[8,3,4096]{2,1,0:T(4,128)(2,1)}), bf16[8,3,4096]{2,1,0:T(4,128)(2,1)S(1)}, u32[]{:S(2)}, u32[]{:S(2)}) async-start(bf16[8,3,4096]{2,1,0:T(4,128)(2,1)} %copy.46), calls=%async_computation | async-start | bytes 524288 | tf_op jit(solution)/shard_map/while/body/eval_jaxpr/all_to_all | solution.py:97
  746.0 7.1 collective-permute-start
  754.9 13.1 %all-to-all-start = ((bf16[8,3,4096]{2,1,0:T(4,128)(2,1)}), bf16[8,3,4096]{2,1,0:T(4,128)(2,1)S(1)}, u32[]{:S(2)}, u32[]{:S(2)}) async-start(bf16[8,3,4096]{2,1,0:T(4,128)(2,1)} %copy.46), calls=%async_computation | async-start | bytes 524288 | tf_op jit(solution)/shard_map/while/body/eval_jaxpr/all_to_all | solution.py:97
  789.3 7.1 collective-permute-start
  798.3 13.1 %all-to-all-start = ((bf16[8,3,4096]{2,1,0:T(4,128)(2,1)}), bf16[8,3,4096]{2,1,0:T(4,128)(2,1)S(1)}, u32[]{:S(2)}, u32[]{:S(2)}) async-start(bf16[8,3,4096]{2,1,0:T(4,128)(2,1)} %copy.46), calls=%async_computation | async-start | bytes 524288 | tf_op jit(solution)/shard_map/while/body/eval_jaxpr/all_to_all | solution.py:97
  832.6 7.1 collective-permute-start
  841.6 13.1 %all-to-all-start = ((bf16[8,3,4096]{2,1,0:T(4,128)(2,1)}), bf16[8,3,4096]{2,1,0:T(4,128)(2,1)S(1)}, u32[]{:S(2)}, u32[]{:S(2)}) async-start(bf16[8,3,4096]{2,1,0:T(4,128)(2,1)} %copy.46), calls=%async_computation | async-start | bytes 524288 | tf_op jit(solution)/shard_map/while/body/eval_jaxpr/all_to_all | solution.py:97
  876.0 7.1 collective-permute-start
  885.0 13.1 %all-to-all-start = ((bf16[8,3,4096]{2,1,0:T(4,128)(2,1)}), bf16[8,3,4096]{2,1,0:T(4,128)(2,1)S(1)}, u32[]{:S(2)}, u32[]{:S(2)}) async-start(bf16[8,3,4096]{2,1,0:T(4,128)(2,1)} %copy.46), calls=%async_computation | async-start | bytes 524288 | tf_op jit(solution)/shard_map/while/body/eval_jaxpr/all_to_all | solution.py:97
  919.3 6.2 collective-permute-start
  (28 other events, 117.1 us)
where the time goes:
time: 933 us; the launch traced here: 926 us
  waiting for transfers between devices  382 us (41%)
  blocking collectives  231 us (25%)
  matrix products  173 us (19%)
  starting transfers between devices  95.7 us (10%)
  local copies, waits for them, and re-layouts  40.7 us (4%)
    all_to_all x19, blocking collectives, tick(): lax.all_to_all(back.reshape(expert_count, capacity, model_width), 'expert...  231 us
    all_to_all x19, waiting for transfers between devices, tick(): lax.all_to_all(grad_rows, 'expert', split_axis=0, concat_axis=0, tiled=True)  183 us
    ppermute x19, waiting for transfers between devices, passed_along(): return lax.ppermute(x, axis, pairs)  127 us
    all_to_all x1, waiting for transfers between devices, on_device(): lax.all_to_all(outgoing, 'expert', split_axis=1, concat_axis=1, tiled=True)  71.5 us
    all_to_all x19, starting transfers between devices, tick(): lax.all_to_all(grad_rows, 'expert', split_axis=0, concat_axis=0, tiled=True)  64.8 us
    dot_general x16, matrix products, backward_rows(): lax.dot_general(grad_block, down_slice, contract, preferred_element_type=...  56.4 us
    dot_general x16, matrix products, backward_rows(): lax.dot_general(dgate, gate_slice, contract, preferred_element_type=jnp.f...  34.3 us
    dot_general x16, matrix products, backward_rows(): lax.dot_general(dup, up_slice, contract, preferred_element_type=jnp.float32)  32.3 us
  transfers between devices with their start and end apart: 39, of which 39 were waited for; matrix products, arithmetic and copies ran while one was open for 0% of the time, Pallas kernels for 0%

commit v1 on v0

--- a/solution.py
+++ b/solution.py
@@ -5,6 +5,7 @@
 
 EXPERTS = 8
 CAP = 3
+CHUNK = 4
 
 
 def passed_along(x, axis, by):
@@ -39,6 +40,8 @@
     shards = expert_count // EXPERTS
     capacity = CAP
     slot_rows = expert_count * capacity
+    chunk = CHUNK if micro_count % CHUNK == 0 else 1
+    chunk_count = micro_count // chunk
     contract = (((1,), (1,)), ((), ()))
     selected = selection(expert_ids[0], capacity)
     dispatch = jnp.sum(selected, axis=2).astype(jnp.bfloat16)
@@ -65,70 +68,57 @@
         total = total + lax.dot_general(dup, up_slice, contract, preferred_element_type=jnp.float32)
         return total.astype(jnp.bfloat16)
 
-    zeros_back = jnp.zeros((slot_rows, model_width), jnp.bfloat16)
     outgoing = spread(
         jnp.einsum("mtec,mtd->mecd", dispatch, inputs, preferred_element_type=jnp.float32)
     )
     received = lax.all_to_all(outgoing, "expert", split_axis=1, concat_axis=1, tiled=True)
-    item_count = received.shape[0]
     row_block = received.reshape(-1, model_width)
     pre_gate = jnp.dot(row_block, gate_slice, preferred_element_type=jnp.float32)
     pre_up = jnp.dot(row_block, up_slice, preferred_element_type=jnp.float32)
     sigmoid_gate = jax.nn.sigmoid(pre_gate)
     act = pre_gate * sigmoid_gate
     coef = pre_up * (sigmoid_gate * (1.0 + pre_gate * (1.0 - sigmoid_gate)))
-    act, coef = (act, coef)
-    saved = jnp.stack([act, coef]).reshape(2, item_count, slot_rows, hidden)
-    act_all = saved[0]
-    coef_all = saved[1]
+    act_all = act.reshape(micro_count, slot_rows, hidden)
+    coef_all = coef.reshape(micro_count, slot_rows, hidden)
 
     def tick(tick_index, state_pair):
         incoming, results = state_pair
-        micro_index = tick_index - (section_count - 1 - section_index)
-        active = (micro_index >= 0) & (micro_index < micro_count)
-        micro_slot = jnp.clip(micro_index, 0, micro_count - 1)
-        top_grad = lax.dynamic_index_in_dim(out_grad, micro_slot, 0, keepdims=False)
+        chunk_index = tick_index - (section_count - 1 - section_index)
+        active = (chunk_index >= 0) & (chunk_index < chunk_count)
+        start = jnp.clip(chunk_index, 0, chunk_count - 1) * chunk
+        top_grad = lax.dynamic_slice_in_dim(out_grad, start, chunk, 0)
         grad_out = jnp.where(section_index == section_count - 1, top_grad, incoming)
-        dispatch_micro = lax.dynamic_index_in_dim(dispatch, micro_slot, 0, keepdims=False)
-        combine_micro = lax.dynamic_index_in_dim(combine, micro_slot, 0, keepdims=False)
+        dispatch_chunk = lax.dynamic_slice_in_dim(dispatch, start, chunk, 0)
+        combine_chunk = lax.dynamic_slice_in_dim(combine, start, chunk, 0)
         grad_rows = spread(
-            jnp.einsum("tec,td->ecd", dispatch_micro, grad_out, preferred_element_type=jnp.float32)
+            jnp.einsum("mtec,mtd->mecd", dispatch_chunk, grad_out, preferred_element_type=jnp.float32)
         )
-        arrived = lax.all_to_all(
-            grad_rows, "expert", split_axis=0, concat_axis=0, tiled=True
-        ).reshape(slot_rows, model_width)
-
-        def local_saved(row_block):
-            act = lax.dynamic_index_in_dim(act_all, micro_slot, 0, keepdims=False)
-            coef = lax.dynamic_index_in_dim(coef_all, micro_slot, 0, keepdims=False)
-            return backward_rows(row_block, act, coef)
-
-        def skip_saved(row_block):
-            return zeros_back
-
-        back = lax.cond(active, local_saved, skip_saved, arrived)
+        arrived = lax.all_to_all(grad_rows, "expert", split_axis=1, concat_axis=1, tiled=True)
+        act_chunk = lax.dynamic_slice_in_dim(act_all, start, chunk, 0).reshape(-1, hidden)
+        coef_chunk = lax.dynamic_slice_in_dim(coef_all, start, chunk, 0).reshape(-1, hidden)
+        back = backward_rows(arrived.reshape(-1, model_width), act_chunk, coef_chunk)
         returned = lax.all_to_all(
-            back.reshape(expert_count, capacity, model_width),
+            back.reshape(chunk, expert_count, capacity, model_width),
             "expert",
-            split_axis=0,
-            concat_axis=0,
+            split_axis=1,
+            concat_axis=1,
             tiled=True,
         )
-        returned = returned.reshape(EXPERTS, shards, capacity, model_width)
+        returned = returned.reshape(chunk, EXPERTS, shards, capacity, model_width)
         mixed = jnp.einsum(
-            "tec,ekcd->td", combine_micro, returned, preferred_element_type=jnp.float32
+            "mtec,mekcd->mtd", combine_chunk, returned, preferred_element_type=jnp.float32
         )
         grad_in = (grad_out.astype(jnp.float32) + mixed).astype(jnp.bfloat16)
-        updated = lax.dynamic_update_index_in_dim(results, grad_in, micro_slot, 0)
+        updated = lax.dynamic_update_slice_in_dim(results, grad_in, start, 0)
         results = jnp.where(active, updated, results)
         passed = passed_along(grad_in, "section", -1)
         return (passed, results)
 
     initial = (
-        jnp.zeros((token_count, model_width), jnp.bfloat16),
+        jnp.zeros((chunk, token_count, model_width), jnp.bfloat16),
         jnp.zeros((micro_count, token_count, model_width), jnp.bfloat16),
     )
-    final_state = lax.fori_loop(0, micro_count + section_count - 1, tick, initial)
+    final_state = lax.fori_loop(0, chunk_count + section_count - 1, tick, initial)
     return final_state[1][None]
 
 

time: 933 us -> 643 us (0.69)
  blocking collectives: 231 us -> 0 us
  matrix products: 173 us -> 83.9 us
  waiting for transfers between devices: 382 us -> 421 us
  starting transfers between devices: 95.7 us -> 65.1 us
  local copies, waits for them, and re-layouts: 40.7 us -> 67.3 us
    all_to_all x19 -> x0, blocking collectives: 231 us -> none  [tick(): lax.all_to_all(back.reshape(expert_count, capacity, model_width), 'expert...]
    all_to_all x19 -> x14, waiting for transfers between devices: 183 us -> 286 us  [the longest x7 146 us: tick(): lax.all_to_all(back.reshape(chunk, expert_count, capacity, model_width),...]
    ppermute x19 -> x7, waiting for transfers between devices: 127 us -> 64.2 us  [passed_along(): return lax.ppermute(x, axis, pairs)]
    dot_general x16 -> x7, matrix products: 56.4 us -> 26.3 us  [backward_rows(): lax.dot_general(grad_block, down_slice, contract, preferred_element_type=...]
    dot_general x16 -> x7, matrix products: 34.3 us -> 9.65 us  [backward_rows(): lax.dot_general(dgate, gate_slice, contract, preferred_element_type=jnp.f...]
    dot_general x16 -> x7, matrix products: 32.3 us -> 9.73 us  [backward_rows(): lax.dot_general(dup, up_slice, contract, preferred_element_type=jnp.float32)]
    ppermute x19 -> x7, starting transfers between devices: 24.5 us -> 8.96 us  [passed_along(): return lax.ppermute(x, axis, pairs)]
    all_to_all x19 -> x14, starting transfers between devices: 64.8 us -> 49.6 us  [the longest x7 24.8 us: tick(): lax.all_to_all(grad_rows, 'expert', split_axis=1, concat_axis=1, tiled=True)]
  transfers between devices with their start and end apart: 39 -> 22, of which waited for: 39 -> 22; matrix products, arithmetic and copies ran while one was open for 0% -> 1% of each run, Pallas kernels for 0% -> 0%
where the time goes in v1:
time: 643 us; the launch traced here: 641 us
  waiting for transfers between devices  421 us (65%)
  matrix products  83.9 us (13%)
  local copies, waits for them, and re-layouts  67.3 us (10%)
  starting transfers between devices  65.1 us (10%)
    all_to_all x7, waiting for transfers between devices, tick(): lax.all_to_all(back.reshape(chunk, expert_count, capacity, model_width),...  146 us
    all_to_all x7, waiting for transfers between devices, tick(): lax.all_to_all(grad_rows, 'expert', split_axis=1, concat_axis=1, tiled=True)  139 us
    all_to_all x1, waiting for transfers between devices, on_device(): lax.all_to_all(outgoing, 'expert', split_axis=1, concat_axis=1, tiled=True)  70.8 us
    ppermute x7, waiting for transfers between devices, passed_along(): return lax.ppermute(x, axis, pairs)  64.2 us
    dot_general x7, matrix products, backward_rows(): lax.dot_general(grad_block, down_slice, contract, preferred_element_type=...  26.3 us
    all_to_all x7, starting transfers between devices, tick(): lax.all_to_all(grad_rows, 'expert', split_axis=1, concat_axis=1, tiled=True)  24.8 us
    all_to_all x7, starting transfers between devices, tick(): lax.all_to_all(back.reshape(chunk, expert_count, capacity, model_width),...  24.8 us
    dot_general x7, matrix products, tick(): jnp.einsum('mtec,mekcd->mtd', combine_chunk, returned, preferred_element_...  18.8 us
  transfers between devices with their start and end apart: 22, of which 22 were waited for; matrix products, arithmetic and copies ran while one was open for 1% of the time, Pallas kernels for 0%

profile of v1, /device:TPU:0, one launch (start us, length us, event | category | flops | bytes accessed | tf_op | source)
XLA Modules:
  0.0 640.6 jit_solution(13273977673544917966)
XLA Ops:
  6.6 6.5 %all-to-all-start.2 = ((bf16[16,8,3,4096]{3,0,2,1:T(8,128)(2,1)}), bf16[16,8,3,4096]{3,0,2,1:T(8,128)(2,1)}, u32[]{:S(2)}, u32[]{:S(2)}) async-start(bf16[16,8,3,4096]{3,0,2,1:T(8,128)(2,1)} %copy.40), calls=%async_computation.2 | async-start | bytes 6291456 | tf_op jit(solution)/shard_map/all_to_all | solution.py:74
  13.9 70.8 %all-to-all-done.2 = bf16[16,8,3,4096]{3,0,2,1:T(8,128)(2,1)} async-done(((bf16[16,8,3,4096]{3,0,2,1:T(8,128)(2,1)}), bf16[16,8,3,4096]{3,0,2,1:T(8,128)(2,1)}, u32[]{:S(2)}, u32[]{:S(2)}) %all-to-all-start.2) | async-done | bytes 3145760 | tf_op jit(solution)/shard_map/all_to_all | solution.py:74
  84.7 6.5 %copy.41 = bf16[16,8,3,4096]{3,2,1,0:T(4,128)(2,1)} copy(bf16[16,8,3,4096]{3,0,2,1:T(8,128)(2,1)} %all-to-all-done.2) | data formatting | bytes 6291456 | tf_op jit(solution)/shard_map/all_to_all | solution.py:74
  91.3 7.4 %reshape.78 = bf16[384,4096]{1,0:T(8,128)(2,1)} reshape(bf16[16,8,3,4096]{3,2,1,0:T(4,128)(2,1)} %copy.41) | data formatting | bytes 6291456 | tf_op jit(solution)/shard_map/reshape | solution.py:75
  98.7 5.2 fusion.13
  107.9 532.7 %while.17 = (s32[]{:T(128)}, bf16[4,8,4096]{2,1,0:T(8,128)(2,1)S(1)}, bf16[16,8,4096]{2,1,0:T(8,128)(2,1)}, pred[]{:T(512)}, s32[]{:T(128)}, /*index=5*/bf16[16,...) while((s32[]{:T(128)}, ...), condition=%wide.region_5.6_spmd, body=%wide.region_4.5_spmd.sunk | while | flops 1222705152 | bytes 75862064 | solution.py:121
  111.1 3.5 all-to-all-start
  115.6 19.9 %all-to-all-done = bf16[4,8,3,4096]{3,0,2,1:T(4,128)(2,1)S(1)} async-done(((bf16[4,8,3,4096]{3,0,2,1:T(4,128)(2,1)}), bf16[4,8,3,4096]{3,0,2,1:T(4,128)(2,1)S(1)}, u32[]{:S(2)}, u32[]{:S(2)}) %all-to-all-start) | async-done | bytes 786464 | tf_op jit(solution)/shard_map/while/body/eval_jaxpr/all_to_all | solution.py:96
  137.0 3.8 fusion.53
  146.5 3.5 all-to-all-start.1
  150.1 20.9 %all-to-all-done.1 = bf16[4,8,3,4096]{3,0,2,1:T(4,128)(2,1)S(1)} async-done(((bf16[4,8,3,4096]{3,0,2,1:T(4,128)(2,1)}), bf16[4,8,3,4096]{3,0,2,1:T(4,128)(2,1)S(1)}, u32[]{:S(2)}, u32[]{:S(2)}) %all-to-all-start.1) | async-done | bytes 786464 | tf_op jit(solution)/shard_map/while/body/eval_jaxpr/all_to_all | solution.py:100
  175.0 8.4 %collective-permute-done = bf16[4,8,4096]{2,1,0:T(8,128)(2,1)S(1)} collective-permute-done((bf16[4,8,4096]{2,1,0:T(8,128)(2,1)S(1)}, bf16[4,8,4096]{2,1,0:T(8,128)(2,1)S(1)}, u32[]{:S(2)}, u32[]{:S(2)}) %collective-permute-start) | collective-permute-done | bytes 262176 | tf_op jit(solution)/shard_map/while/body/eval_jaxpr/ppermute | solution.py:14
  186.4 3.5 all-to-all-start
  191.0 19.9 %all-to-all-done = bf16[4,8,3,4096]{3,0,2,1:T(4,128)(2,1)S(1)} async-done(((bf16[4,8,3,4096]{3,0,2,1:T(4,128)(2,1)}), bf16[4,8,3,4096]{3,0,2,1:T(4,128)(2,1)S(1)}, u32[]{:S(2)}, u32[]{:S(2)}) %all-to-all-start) | async-done | bytes 786464 | tf_op jit(solution)/shard_map/while/body/eval_jaxpr/all_to_all | solution.py:96
  212.3 3.8 fusion.53
  221.9 3.5 all-to-all-start.1
  225.4 20.9 %all-to-all-done.1 = bf16[4,8,3,4096]{3,0,2,1:T(4,128)(2,1)S(1)} async-done(((bf16[4,8,3,4096]{3,0,2,1:T(4,128)(2,1)}), bf16[4,8,3,4096]{3,0,2,1:T(4,128)(2,1)S(1)}, u32[]{:S(2)}, u32[]{:S(2)}) %all-to-all-start.1) | async-done | bytes 786464 | tf_op jit(solution)/shard_map/while/body/eval_jaxpr/all_to_all | solution.py:100
  250.3 9.1 %collective-permute-done = bf16[4,8,4096]{2,1,0:T(8,128)(2,1)S(1)} collective-permute-done((bf16[4,8,4096]{2,1,0:T(8,128)(2,1)S(1)}, bf16[4,8,4096]{2,1,0:T(8,128)(2,1)S(1)}, u32[]{:S(2)}, u32[]{:S(2)}) %collective-permute-start) | collective-permute-done | bytes 262176 | tf_op jit(solution)/shard_map/while/body/eval_jaxpr/ppermute | solution.py:14
  262.4 3.5 all-to-all-start
  266.9 19.9 %all-to-all-done = bf16[4,8,3,4096]{3,0,2,1:T(4,128)(2,1)S(1)} async-done(((bf16[4,8,3,4096]{3,0,2,1:T(4,128)(2,1)}), bf16[4,8,3,4096]{3,0,2,1:T(4,128)(2,1)S(1)}, u32[]{:S(2)}, u32[]{:S(2)}) %all-to-all-start) | async-done | bytes 786464 | tf_op jit(solution)/shard_map/while/body/eval_jaxpr/all_to_all | solution.py:96
  288.3 3.8 fusion.53
  297.9 3.5 all-to-all-start.1
  301.4 20.9 %all-to-all-done.1 = bf16[4,8,3,4096]{3,0,2,1:T(4,128)(2,1)S(1)} async-done(((bf16[4,8,3,4096]{3,0,2,1:T(4,128)(2,1)}), bf16[4,8,3,4096]{3,0,2,1:T(4,128)(2,1)S(1)}, u32[]{:S(2)}, u32[]{:S(2)}) %all-to-all-start.1) | async-done | bytes 786464 | tf_op jit(solution)/shard_map/while/body/eval_jaxpr/all_to_all | solution.py:100
  326.3 9.3 %collective-permute-done = bf16[4,8,4096]{2,1,0:T(8,128)(2,1)S(1)} collective-permute-done((bf16[4,8,4096]{2,1,0:T(8,128)(2,1)S(1)}, bf16[4,8,4096]{2,1,0:T(8,128)(2,1)S(1)}, u32[]{:S(2)}, u32[]{:S(2)}) %collective-permute-start) | collective-permute-done | bytes 262176 | tf_op jit(solution)/shard_map/while/body/eval_jaxpr/ppermute | solution.py:14
  338.6 3.5 all-to-all-start
  343.2 19.9 %all-to-all-done = bf16[4,8,3,4096]{3,0,2,1:T(4,128)(2,1)S(1)} async-done(((bf16[4,8,3,4096]{3,0,2,1:T(4,128)(2,1)}), bf16[4,8,3,4096]{3,0,2,1:T(4,128)(2,1)S(1)}, u32[]{:S(2)}, u32[]{:S(2)}) %all-to-all-start) | async-done | bytes 786464 | tf_op jit(solution)/shard_map/while/body/eval_jaxpr/all_to_all | solution.py:96
  364.6 3.8 fusion.53
  374.1 3.5 all-to-all-start.1
  377.7 20.9 %all-to-all-done.1 = bf16[4,8,3,4096]{3,0,2,1:T(4,128)(2,1)S(1)} async-done(((bf16[4,8,3,4096]{3,0,2,1:T(4,128)(2,1)}), bf16[4,8,3,4096]{3,0,2,1:T(4,128)(2,1)S(1)}, u32[]{:S(2)}, u32[]{:S(2)}) %all-to-all-start.1) | async-done | bytes 786464 | tf_op jit(solution)/shard_map/while/body/eval_jaxpr/all_to_all | solution.py:100
  402.5 9.3 %collective-permute-done = bf16[4,8,4096]{2,1,0:T(8,128)(2,1)S(1)} collective-permute-done((bf16[4,8,4096]{2,1,0:T(8,128)(2,1)S(1)}, bf16[4,8,4096]{2,1,0:T(8,128)(2,1)S(1)}, u32[]{:S(2)}, u32[]{:S(2)}) %collective-permute-start) | collective-permute-done | bytes 262176 | tf_op jit(solution)/shard_map/while/body/eval_jaxpr/ppermute | solution.py:14
  414.9 3.5 all-to-all-start
  419.4 19.9 %all-to-all-done = bf16[4,8,3,4096]{3,0,2,1:T(4,128)(2,1)S(1)} async-done(((bf16[4,8,3,4096]{3,0,2,1:T(4,128)(2,1)}), bf16[4,8,3,4096]{3,0,2,1:T(4,128)(2,1)S(1)}, u32[]{:S(2)}, u32[]{:S(2)}) %all-to-all-start) | async-done | bytes 786464 | tf_op jit(solution)/shard_map/while/body/eval_jaxpr/all_to_all | solution.py:96
  440.8 3.8 fusion.53
  450.3 3.5 all-to-all-start.1
  453.9 20.9 %all-to-all-done.1 = bf16[4,8,3,4096]{3,0,2,1:T(4,128)(2,1)S(1)} async-done(((bf16[4,8,3,4096]{3,0,2,1:T(4,128)(2,1)}), bf16[4,8,3,4096]{3,0,2,1:T(4,128)(2,1)S(1)}, u32[]{:S(2)}, u32[]{:S(2)}) %all-to-all-start.1) | async-done | bytes 786464 | tf_op jit(solution)/shard_map/while/body/eval_jaxpr/all_to_all | solution.py:100
  478.8 9.3 %collective-permute-done = bf16[4,8,4096]{2,1,0:T(8,128)(2,1)S(1)} collective-permute-done((bf16[4,8,4096]{2,1,0:T(8,128)(2,1)S(1)}, bf16[4,8,4096]{2,1,0:T(8,128)(2,1)S(1)}, u32[]{:S(2)}, u32[]{:S(2)}) %collective-permute-start) | collective-permute-done | bytes 262176 | tf_op jit(solution)/shard_map/while/body/eval_jaxpr/ppermute | solution.py:14
  491.1 3.5 all-to-all-start
  495.7 19.9 %all-to-all-done = bf16[4,8,3,4096]{3,0,2,1:T(4,128)(2,1)S(1)} async-done(((bf16[4,8,3,4096]{3,0,2,1:T(4,128)(2,1)}), bf16[4,8,3,4096]{3,0,2,1:T(4,128)(2,1)S(1)}, u32[]{:S(2)}, u32[]{:S(2)}) %all-to-all-start) | async-done | bytes 786464 | tf_op jit(solution)/shard_map/while/body/eval_jaxpr/all_to_all | solution.py:96
  517.0 3.8 fusion.53
  526.6 3.5 all-to-all-start.1
  530.1 20.9 %all-to-all-done.1 = bf16[4,8,3,4096]{3,0,2,1:T(4,128)(2,1)S(1)} async-done(((bf16[4,8,3,4096]{3,0,2,1:T(4,128)(2,1)}), bf16[4,8,3,4096]{3,0,2,1:T(4,128)(2,1)S(1)}, u32[]{:S(2)}, u32[]{:S(2)}) %all-to-all-start.1) | async-done | bytes 786464 | tf_op jit(solution)/shard_map/while/body/eval_jaxpr/all_to_all | solution.py:100
  555.0 9.3 %collective-permute-done = bf16[4,8,4096]{2,1,0:T(8,128)(2,1)S(1)} collective-permute-done((bf16[4,8,4096]{2,1,0:T(8,128)(2,1)S(1)}, bf16[4,8,4096]{2,1,0:T(8,128)(2,1)S(1)}, u32[]{:S(2)}, u32[]{:S(2)}) %collective-permute-start) | collective-permute-done | bytes 262176 | tf_op jit(solution)/shard_map/while/body/eval_jaxpr/ppermute | solution.py:14
  567.4 3.5 all-to-all-start
  571.9 19.9 %all-to-all-done = bf16[4,8,3,4096]{3,0,2,1:T(4,128)(2,1)S(1)} async-done(((bf16[4,8,3,4096]{3,0,2,1:T(4,128)(2,1)}), bf16[4,8,3,4096]{3,0,2,1:T(4,128)(2,1)S(1)}, u32[]{:S(2)}, u32[]{:S(2)}) %all-to-all-start) | async-done | bytes 786464 | tf_op jit(solution)/shard_map/while/body/eval_jaxpr/all_to_all | solution.py:96
  593.3 3.8 fusion.53
  602.8 3.5 all-to-all-start.1
  606.4 20.9 %all-to-all-done.1 = bf16[4,8,3,4096]{3,0,2,1:T(4,128)(2,1)S(1)} async-done(((bf16[4,8,3,4096]{3,0,2,1:T(4,128)(2,1)}), bf16[4,8,3,4096]{3,0,2,1:T(4,128)(2,1)S(1)}, u32[]{:S(2)}, u32[]{:S(2)}) %all-to-all-start.1) | async-done | bytes 786464 | tf_op jit(solution)/shard_map/while/body/eval_jaxpr/all_to_all | solution.py:100
  631.2 9.3 %collective-permute-done = bf16[4,8,4096]{2,1,0:T(8,128)(2,1)S(1)} collective-permute-done((bf16[4,8,4096]{2,1,0:T(8,128)(2,1)S(1)}, bf16[4,8,4096]{2,1,0:T(8,128)(2,1)S(1)}, u32[]{:S(2)}, u32[]{:S(2)}) %collective-permute-start) | collective-permute-done | bytes 262176 | tf_op jit(solution)/shard_map/while/body/eval_jaxpr/ppermute | solution.py:14
  (183 shorter events, 116.9 us)
Async XLA Ops:
  6.6 78.1 %all-to-all-start.2 = ((bf16[16,8,3,4096]{3,0,2,1:T(8,128)(2,1)}), bf16[16,8,3,4096]{3,0,2,1:T(8,128)(2,1)}, u32[]{:S(2)}, u32[]{:S(2)}) async-start(bf16[16,8,3,4096]{3,0,2,1:T(8,128)(2,1)} %copy.40), calls=%async_computation.2 | async-start | bytes 6291456 | tf_op jit(solution)/shard_map/all_to_all | solution.py:74
  111.1 24.4 %all-to-all-start = ((bf16[4,8,3,4096]{3,0,2,1:T(4,128)(2,1)}), bf16[4,8,3,4096]{3,0,2,1:T(4,128)(2,1)S(1)}, u32[]{:S(2)}, u32[]{:S(2)}) async-start(bf16[4,8,3,4096]{3,0,2,1:T(4,128)(2,1)} %copy.56), calls=%async_computation | async-start | bytes 1572864 | tf_op jit(solution)/shard_map/while/body/eval_jaxpr/all_to_all | solution.py:96
  144.4 39.0 %copy-start.8 = (bf16[16,8,8,3]{1,2,3,0:T(8,128)(2,1)S(1)}, bf16[16,8,8,3]{1,2,3,0:T(8,128)(2,1)}, u32[]{:S(2)}) copy-start(bf16[16,8,8,3]{1,2,3,0:T(8,128)(2,1)} %copy-done.7) | copy-start | bytes 18436 | tf_op jit(solution)/shard_map/while
  144.9 38.5 %copy-start.6 = (f32[16,24,512]{2,1,0:T(8,128)S(1)}, f32[16,24,512]{2,1,0:T(8,128)}, u32[]{:S(2)}) copy-start(f32[16,24,512]{2,1,0:T(8,128)} %copy-done.5) | copy-start | bytes 2359300 | tf_op jit(solution)/shard_map/while
  146.5 24.4 %all-to-all-start.1 = ((bf16[4,8,3,4096]{3,0,2,1:T(4,128)(2,1)}), bf16[4,8,3,4096]{3,0,2,1:T(4,128)(2,1)S(1)}, u32[]{:S(2)}, u32[]{:S(2)}) async-start(bf16[4,8,3,4096]{3,0,2,1:T(4,128)(2,1)} %copy.58), calls=%async_computation.1 | async-start | bytes 1572864 | tf_op jit(solution)/shard_map/while/body/eval_jaxpr/all_to_all | solution.py:100
  173.7 9.7 %collective-permute-start = (bf16[4,8,4096]{2,1,0:T(8,128)(2,1)S(1)}, bf16[4,8,4096]{2,1,0:T(8,128)(2,1)S(1)}, u32[]{:S(2)}, u32[]{:S(2)}) collective-permute-start(bf16[4,8,4096]{2,1,0:T(8,128)(2,1)S(1)} %get-tuple-element.422), channel_id=1, source_target_pairs={{8,0},{16,8},{24,16},{9,1},{17,9},{25,17},{10,2},{18,10},{26,18},{... | collective-permute-start | bytes 786440 | tf_op jit(solution)/shard_map/while/body/eval_jaxpr/ppermute | solution.py:14
  183.4 7.5 %copy-start.5 = (f32[16,24,512]{2,1,0:T(8,128)}, f32[16,24,512]{2,1,0:T(8,128)S(1)}, u32[]{:S(2)}) copy-start(f32[16,24,512]{2,1,0:T(8,128)S(1)} %get-tuple-element.471) | copy-start | bytes 2359300 | tf_op jit(solution)/shard_map/while
  183.4 7.5 %copy-start.7 = (bf16[16,8,8,3]{1,2,3,0:T(8,128)(2,1)}, bf16[16,8,8,3]{1,2,3,0:T(8,128)(2,1)S(1)}, u32[]{:S(2)}) copy-start(bf16[16,8,8,3]{1,2,3,0:T(8,128)(2,1)S(1)} %get-tuple-element.467) | copy-start | bytes 18436 | tf_op jit(solution)/shard_map/while
  186.4 24.4 %all-to-all-start = ((bf16[4,8,3,4096]{3,0,2,1:T(4,128)(2,1)}), bf16[4,8,3,4096]{3,0,2,1:T(4,128)(2,1)S(1)}, u32[]{:S(2)}, u32[]{:S(2)}) async-start(bf16[4,8,3,4096]{3,0,2,1:T(4,128)(2,1)} %copy.56), calls=%async_computation | async-start | bytes 1572864 | tf_op jit(solution)/shard_map/while/body/eval_jaxpr/all_to_all | solution.py:96
  219.7 39.7 %copy-start.8 = (bf16[16,8,8,3]{1,2,3,0:T(8,128)(2,1)S(1)}, bf16[16,8,8,3]{1,2,3,0:T(8,128)(2,1)}, u32[]{:S(2)}) copy-start(bf16[16,8,8,3]{1,2,3,0:T(8,128)(2,1)} %copy-done.7) | copy-start | bytes 18436 | tf_op jit(solution)/shard_map/while
  220.2 39.2 %copy-start.6 = (f32[16,24,512]{2,1,0:T(8,128)S(1)}, f32[16,24,512]{2,1,0:T(8,128)}, u32[]{:S(2)}) copy-start(f32[16,24,512]{2,1,0:T(8,128)} %copy-done.5) | copy-start | bytes 2359300 | tf_op jit(solution)/shard_map/while
  221.9 24.4 %all-to-all-start.1 = ((bf16[4,8,3,4096]{3,0,2,1:T(4,128)(2,1)}), bf16[4,8,3,4096]{3,0,2,1:T(4,128)(2,1)S(1)}, u32[]{:S(2)}, u32[]{:S(2)}) async-start(bf16[4,8,3,4096]{3,0,2,1:T(4,128)(2,1)} %copy.58), calls=%async_computation.1 | async-start | bytes 1572864 | tf_op jit(solution)/shard_map/while/body/eval_jaxpr/all_to_all | solution.py:100
  249.0 10.4 %collective-permute-start = (bf16[4,8,4096]{2,1,0:T(8,128)(2,1)S(1)}, bf16[4,8,4096]{2,1,0:T(8,128)(2,1)S(1)}, u32[]{:S(2)}, u32[]{:S(2)}) collective-permute-start(bf16[4,8,4096]{2,1,0:T(8,128)(2,1)S(1)} %get-tuple-element.422), channel_id=1, source_target_pairs={{8,0},{16,8},{24,16},{9,1},{17,9},{25,17},{10,2},{18,10},{26,18},{... | collective-permute-start | bytes 786440 | tf_op jit(solution)/shard_map/while/body/eval_jaxpr/ppermute | solution.py:14
  259.4 7.5 %copy-start.5 = (f32[16,24,512]{2,1,0:T(8,128)}, f32[16,24,512]{2,1,0:T(8,128)S(1)}, u32[]{:S(2)}) copy-start(f32[16,24,512]{2,1,0:T(8,128)S(1)} %get-tuple-element.471) | copy-start | bytes 2359300 | tf_op jit(solution)/shard_map/while
  259.4 7.5 %copy-start.7 = (bf16[16,8,8,3]{1,2,3,0:T(8,128)(2,1)}, bf16[16,8,8,3]{1,2,3,0:T(8,128)(2,1)S(1)}, u32[]{:S(2)}) copy-start(bf16[16,8,8,3]{1,2,3,0:T(8,128)(2,1)S(1)} %get-tuple-element.467) | copy-start | bytes 18436 | tf_op jit(solution)/shard_map/while
  262.4 24.4 %all-to-all-start = ((bf16[4,8,3,4096]{3,0,2,1:T(4,128)(2,1)}), bf16[4,8,3,4096]{3,0,2,1:T(4,128)(2,1)S(1)}, u32[]{:S(2)}, u32[]{:S(2)}) async-start(bf16[4,8,3,4096]{3,0,2,1:T(4,128)(2,1)} %copy.56), calls=%async_computation | async-start | bytes 1572864 | tf_op jit(solution)/shard_map/while/body/eval_jaxpr/all_to_all | solution.py:96
  295.7 39.9 %copy-start.8 = (bf16[16,8,8,3]{1,2,3,0:T(8,128)(2,1)S(1)}, bf16[16,8,8,3]{1,2,3,0:T(8,128)(2,1)}, u32[]{:S(2)}) copy-start(bf16[16,8,8,3]{1,2,3,0:T(8,128)(2,1)} %copy-done.7) | copy-start | bytes 18436 | tf_op jit(solution)/shard_map/while
  296.2 39.4 %copy-start.6 = (f32[16,24,512]{2,1,0:T(8,128)S(1)}, f32[16,24,512]{2,1,0:T(8,128)}, u32[]{:S(2)}) copy-start(f32[16,24,512]{2,1,0:T(8,128)} %copy-done.5) | copy-start | bytes 2359300 | tf_op jit(solution)/shard_map/while
  297.9 24.4 %all-to-all-start.1 = ((bf16[4,8,3,4096]{3,0,2,1:T(4,128)(2,1)}), bf16[4,8,3,4096]{3,0,2,1:T(4,128)(2,1)S(1)}, u32[]{:S(2)}, u32[]{:S(2)}) async-start(bf16[4,8,3,4096]{3,0,2,1:T(4,128)(2,1)} %copy.58), calls=%async_computation.1 | async-start | bytes 1572864 | tf_op jit(solution)/shard_map/while/body/eval_jaxpr/all_to_all | solution.py:100
  325.0 10.6 %collective-permute-start = (bf16[4,8,4096]{2,1,0:T(8,128)(2,1)S(1)}, bf16[4,8,4096]{2,1,0:T(8,128)(2,1)S(1)}, u32[]{:S(2)}, u32[]{:S(2)}) collective-permute-start(bf16[4,8,4096]{2,1,0:T(8,128)(2,1)S(1)} %get-tuple-element.422), channel_id=1, source_target_pairs={{8,0},{16,8},{24,16},{9,1},{17,9},{25,17},{10,2},{18,10},{26,18},{... | collective-permute-start | bytes 786440 | tf_op jit(solution)/shard_map/while/body/eval_jaxpr/ppermute | solution.py:14
  335.6 7.5 %copy-start.5 = (f32[16,24,512]{2,1,0:T(8,128)}, f32[16,24,512]{2,1,0:T(8,128)S(1)}, u32[]{:S(2)}) copy-start(f32[16,24,512]{2,1,0:T(8,128)S(1)} %get-tuple-element.471) | copy-start | bytes 2359300 | tf_op jit(solution)/shard_map/while
  335.6 7.5 %copy-start.7 = (bf16[16,8,8,3]{1,2,3,0:T(8,128)(2,1)}, bf16[16,8,8,3]{1,2,3,0:T(8,128)(2,1)S(1)}, u32[]{:S(2)}) copy-start(bf16[16,8,8,3]{1,2,3,0:T(8,128)(2,1)S(1)} %get-tuple-element.467) | copy-start | bytes 18436 | tf_op jit(solution)/shard_map/while
  338.6 24.4 %all-to-all-start = ((bf16[4,8,3,4096]{3,0,2,1:T(4,128)(2,1)}), bf16[4,8,3,4096]{3,0,2,1:T(4,128)(2,1)S(1)}, u32[]{:S(2)}, u32[]{:S(2)}) async-start(bf16[4,8,3,4096]{3,0,2,1:T(4,128)(2,1)} %copy.56), calls=%async_computation | async-start | bytes 1572864 | tf_op jit(solution)/shard_map/while/body/eval_jaxpr/all_to_all | solution.py:96
  371.9 39.9 %copy-start.8 = (bf16[16,8,8,3]{1,2,3,0:T(8,128)(2,1)S(1)}, bf16[16,8,8,3]{1,2,3,0:T(8,128)(2,1)}, u32[]{:S(2)}) copy-start(bf16[16,8,8,3]{1,2,3,0:T(8,128)(2,1)} %copy-done.7) | copy-start | bytes 18436 | tf_op jit(solution)/shard_map/while
  372.5 39.4 %copy-start.6 = (f32[16,24,512]{2,1,0:T(8,128)S(1)}, f32[16,24,512]{2,1,0:T(8,128)}, u32[]{:S(2)}) copy-start(f32[16,24,512]{2,1,0:T(8,128)} %copy-done.5) | copy-start | bytes 2359300 | tf_op jit(solution)/shard_map/while
  374.1 24.4 %all-to-all-start.1 = ((bf16[4,8,3,4096]{3,0,2,1:T(4,128)(2,1)}), bf16[4,8,3,4096]{3,0,2,1:T(4,128)(2,1)S(1)}, u32[]{:S(2)}, u32[]{:S(2)}) async-start(bf16[4,8,3,4096]{3,0,2,1:T(4,128)(2,1)} %copy.58), calls=%async_computation.1 | async-start | bytes 1572864 | tf_op jit(solution)/shard_map/while/body/eval_jaxpr/all_to_all | solution.py:100
  401.2 10.6 %collective-permute-start = (bf16[4,8,4096]{2,1,0:T(8,128)(2,1)S(1)}, bf16[4,8,4096]{2,1,0:T(8,128)(2,1)S(1)}, u32[]{:S(2)}, u32[]{:S(2)}) collective-permute-start(bf16[4,8,4096]{2,1,0:T(8,128)(2,1)S(1)} %get-tuple-element.422), channel_id=1, source_target_pairs={{8,0},{16,8},{24,16},{9,1},{17,9},{25,17},{10,2},{18,10},{26,18},{... | collective-permute-start | bytes 786440 | tf_op jit(solution)/shard_map/while/body/eval_jaxpr/ppermute | solution.py:14
  411.9 7.5 %copy-start.5 = (f32[16,24,512]{2,1,0:T(8,128)}, f32[16,24,512]{2,1,0:T(8,128)S(1)}, u32[]{:S(2)}) copy-start(f32[16,24,512]{2,1,0:T(8,128)S(1)} %get-tuple-element.471) | copy-start | bytes 2359300 | tf_op jit(solution)/shard_map/while
  411.9 7.5 %copy-start.7 = (bf16[16,8,8,3]{1,2,3,0:T(8,128)(2,1)}, bf16[16,8,8,3]{1,2,3,0:T(8,128)(2,1)S(1)}, u32[]{:S(2)}) copy-start(bf16[16,8,8,3]{1,2,3,0:T(8,128)(2,1)S(1)} %get-tuple-element.467) | copy-start | bytes 18436 | tf_op jit(solution)/shard_map/while
  414.9 24.4 %all-to-all-start = ((bf16[4,8,3,4096]{3,0,2,1:T(4,128)(2,1)}), bf16[4,8,3,4096]{3,0,2,1:T(4,128)(2,1)S(1)}, u32[]{:S(2)}, u32[]{:S(2)}) async-start(bf16[4,8,3,4096]{3,0,2,1:T(4,128)(2,1)} %copy.56), calls=%async_computation | async-start | bytes 1572864 | tf_op jit(solution)/shard_map/while/body/eval_jaxpr/all_to_all | solution.py:96
  448.2 39.9 %copy-start.8 = (bf16[16,8,8,3]{1,2,3,0:T(8,128)(2,1)S(1)}, bf16[16,8,8,3]{1,2,3,0:T(8,128)(2,1)}, u32[]{:S(2)}) copy-start(bf16[16,8,8,3]{1,2,3,0:T(8,128)(2,1)} %copy-done.7) | copy-start | bytes 18436 | tf_op jit(solution)/shard_map/while
  448.7 39.4 %copy-start.6 = (f32[16,24,512]{2,1,0:T(8,128)S(1)}, f32[16,24,512]{2,1,0:T(8,128)}, u32[]{:S(2)}) copy-start(f32[16,24,512]{2,1,0:T(8,128)} %copy-done.5) | copy-start | bytes 2359300 | tf_op jit(solution)/shard_map/while
  450.3 24.4 %all-to-all-start.1 = ((bf16[4,8,3,4096]{3,0,2,1:T(4,128)(2,1)}), bf16[4,8,3,4096]{3,0,2,1:T(4,128)(2,1)S(1)}, u32[]{:S(2)}, u32[]{:S(2)}) async-start(bf16[4,8,3,4096]{3,0,2,1:T(4,128)(2,1)} %copy.58), calls=%async_computation.1 | async-start | bytes 1572864 | tf_op jit(solution)/shard_map/while/body/eval_jaxpr/all_to_all | solution.py:100
  477.5 10.6 %collective-permute-start = (bf16[4,8,4096]{2,1,0:T(8,128)(2,1)S(1)}, bf16[4,8,4096]{2,1,0:T(8,128)(2,1)S(1)}, u32[]{:S(2)}, u32[]{:S(2)}) collective-permute-start(bf16[4,8,4096]{2,1,0:T(8,128)(2,1)S(1)} %get-tuple-element.422), channel_id=1, source_target_pairs={{8,0},{16,8},{24,16},{9,1},{17,9},{25,17},{10,2},{18,10},{26,18},{... | collective-permute-start | bytes 786440 | tf_op jit(solution)/shard_map/while/body/eval_jaxpr/ppermute | solution.py:14
  488.1 7.5 %copy-start.5 = (f32[16,24,512]{2,1,0:T(8,128)}, f32[16,24,512]{2,1,0:T(8,128)S(1)}, u32[]{:S(2)}) copy-start(f32[16,24,512]{2,1,0:T(8,128)S(1)} %get-tuple-element.471) | copy-start | bytes 2359300 | tf_op jit(solution)/shard_map/while
  488.1 7.5 %copy-start.7 = (bf16[16,8,8,3]{1,2,3,0:T(8,128)(2,1)}, bf16[16,8,8,3]{1,2,3,0:T(8,128)(2,1)S(1)}, u32[]{:S(2)}) copy-start(bf16[16,8,8,3]{1,2,3,0:T(8,128)(2,1)S(1)} %get-tuple-element.467) | copy-start | bytes 18436 | tf_op jit(solution)/shard_map/while
  491.1 24.4 %all-to-all-start = ((bf16[4,8,3,4096]{3,0,2,1:T(4,128)(2,1)}), bf16[4,8,3,4096]{3,0,2,1:T(4,128)(2,1)S(1)}, u32[]{:S(2)}, u32[]{:S(2)}) async-start(bf16[4,8,3,4096]{3,0,2,1:T(4,128)(2,1)} %copy.56), calls=%async_computation | async-start | bytes 1572864 | tf_op jit(solution)/shard_map/while/body/eval_jaxpr/all_to_all | solution.py:96
  524.4 39.9 %copy-start.8 = (bf16[16,8,8,3]{1,2,3,0:T(8,128)(2,1)S(1)}, bf16[16,8,8,3]{1,2,3,0:T(8,128)(2,1)}, u32[]{:S(2)}) copy-start(bf16[16,8,8,3]{1,2,3,0:T(8,128)(2,1)} %copy-done.7) | copy-start | bytes 18436 | tf_op jit(solution)/shard_map/while
  524.9 39.4 %copy-start.6 = (f32[16,24,512]{2,1,0:T(8,128)S(1)}, f32[16,24,512]{2,1,0:T(8,128)}, u32[]{:S(2)}) copy-start(f32[16,24,512]{2,1,0:T(8,128)} %copy-done.5) | copy-start | bytes 2359300 | tf_op jit(solution)/shard_map/while
  526.6 24.4 %all-to-all-start.1 = ((bf16[4,8,3,4096]{3,0,2,1:T(4,128)(2,1)}), bf16[4,8,3,4096]{3,0,2,1:T(4,128)(2,1)S(1)}, u32[]{:S(2)}, u32[]{:S(2)}) async-start(bf16[4,8,3,4096]{3,0,2,1:T(4,128)(2,1)} %copy.58), calls=%async_computation.1 | async-start | bytes 1572864 | tf_op jit(solution)/shard_map/while/body/eval_jaxpr/all_to_all | solution.py:100
  553.7 10.6 %collective-permute-start = (bf16[4,8,4096]{2,1,0:T(8,128)(2,1)S(1)}, bf16[4,8,4096]{2,1,0:T(8,128)(2,1)S(1)}, u32[]{:S(2)}, u32[]{:S(2)}) collective-permute-start(bf16[4,8,4096]{2,1,0:T(8,128)(2,1)S(1)} %get-tuple-element.422), channel_id=1, source_target_pairs={{8,0},{16,8},{24,16},{9,1},{17,9},{25,17},{10,2},{18,10},{26,18},{... | collective-permute-start | bytes 786440 | tf_op jit(solution)/shard_map/while/body/eval_jaxpr/ppermute | solution.py:14
  564.3 7.5 %copy-start.5 = (f32[16,24,512]{2,1,0:T(8,128)}, f32[16,24,512]{2,1,0:T(8,128)S(1)}, u32[]{:S(2)}) copy-start(f32[16,24,512]{2,1,0:T(8,128)S(1)} %get-tuple-element.471) | copy-start | bytes 2359300 | tf_op jit(solution)/shard_map/while
  564.3 7.5 %copy-start.7 = (bf16[16,8,8,3]{1,2,3,0:T(8,128)(2,1)}, bf16[16,8,8,3]{1,2,3,0:T(8,128)(2,1)S(1)}, u32[]{:S(2)}) copy-start(bf16[16,8,8,3]{1,2,3,0:T(8,128)(2,1)S(1)} %get-tuple-element.467) | copy-start | bytes 18436 | tf_op jit(solution)/shard_map/while
  567.4 24.4 %all-to-all-start = ((bf16[4,8,3,4096]{3,0,2,1:T(4,128)(2,1)}), bf16[4,8,3,4096]{3,0,2,1:T(4,128)(2,1)S(1)}, u32[]{:S(2)}, u32[]{:S(2)}) async-start(bf16[4,8,3,4096]{3,0,2,1:T(4,128)(2,1)} %copy.56), calls=%async_computation | async-start | bytes 1572864 | tf_op jit(solution)/shard_map/while/body/eval_jaxpr/all_to_all | solution.py:96
  600.6 39.9 %copy-start.8 = (bf16[16,8,8,3]{1,2,3,0:T(8,128)(2,1)S(1)}, bf16[16,8,8,3]{1,2,3,0:T(8,128)(2,1)}, u32[]{:S(2)}) copy-start(bf16[16,8,8,3]{1,2,3,0:T(8,128)(2,1)} %copy-done.7) | copy-start | bytes 18436 | tf_op jit(solution)/shard_map/while
  601.2 39.4 %copy-start.6 = (f32[16,24,512]{2,1,0:T(8,128)S(1)}, f32[16,24,512]{2,1,0:T(8,128)}, u32[]{:S(2)}) copy-start(f32[16,24,512]{2,1,0:T(8,128)} %copy-done.5) | copy-start | bytes 2359300 | tf_op jit(solution)/shard_map/while
  602.8 24.4 %all-to-all-start.1 = ((bf16[4,8,3,4096]{3,0,2,1:T(4,128)(2,1)}), bf16[4,8,3,4096]{3,0,2,1:T(4,128)(2,1)S(1)}, u32[]{:S(2)}, u32[]{:S(2)}) async-start(bf16[4,8,3,4096]{3,0,2,1:T(4,128)(2,1)} %copy.58), calls=%async_computation.1 | async-start | bytes 1572864 | tf_op jit(solution)/shard_map/while/body/eval_jaxpr/all_to_all | solution.py:100
  629.9 10.6 %collective-permute-start = (bf16[4,8,4096]{2,1,0:T(8,128)(2,1)S(1)}, bf16[4,8,4096]{2,1,0:T(8,128)(2,1)S(1)}, u32[]{:S(2)}, u32[]{:S(2)}) collective-permute-start(bf16[4,8,4096]{2,1,0:T(8,128)(2,1)S(1)} %get-tuple-element.422), channel_id=1, source_target_pairs={{8,0},{16,8},{24,16},{9,1},{17,9},{25,17},{10,2},{18,10},{26,18},{... | collective-permute-start | bytes 786440 | tf_op jit(solution)/shard_map/while/body/eval_jaxpr/ppermute | solution.py:14
  (20 other events, 76.3 us)
